TPU v7x, 32 devices: a whole 2x2x4 slice. The times are simulated.
32 devices in a mesh: region: 4 (over y, x), col: 8 (over z, core).
Axes of the slice: x: 2, y: 2, z: 4, core: 2. Of those that a mesh axis runs over, the one named last changes fastest.
Arguments:
- tiles: float32 [1536, 128, 128], P(('region', 'col')), may hold values from -0.109375 to 0.109375
- tile_rows: int32 [1536], P(('region', 'col')), may hold values from 0 to 1
- tile_cols: int32 [1536], P(('region', 'col')), may hold values from 0 to 15
- tile_count: int32 [32], P(('region', 'col')), may hold values from 12 to 48, as said below
- rhs: float32 [64, 128], P(('region', 'col')), may hold values from -6 to 6
- base_cost: float32 [64, 128], P(('region', 'col')), may hold values from 0.1 to 1
- upper: float32 [64, 128], P(('region', 'col')), may hold values from 0.5 to 4
- primal: float32 [64, 16, 128], P(('region', 'col')), may hold values from 0 to 1
- dual: float32 [64, 16, 128], P(('region', 'col')), may hold values from 0 to 1
- price_levels: float32 [32, 128], replicated, may hold values from 0.5 to 2
- scenario_ids: int32 [16], replicated, may hold values from 0 to 31
Outputs:
- primal_out: float32 [64, 16, 128], P(('region', 'col'))
- dual_out: float32 [64, 16, 128], P(('region', 'col'))
- weight_out: float32 [16], replicated
Inputs may be any that keep to these rules, and one draw needn't show every extreme that they name: `tile_count`: slots at or past a device's count are padding and hold no part of the matrix; in every draw some device has all 48 slots live.
All inputs are finite; a program needn't handle non-finite values.
Results may differ from a plain program's by a relative error of at most 0.0001.
Values sent between devices are 32-bit elements; how exact they have to be, the bound alone decides.
No kernel may reach another device: no remote copies, remote signals or barrier semaphores. Data moves between devices by JAX's collectives and lax.ppermute only.
A program may use at most 64 MiB of HBM per device.

v0:
```python
import jax
import jax.numpy as jnp
from jax import lax
from jax.sharding import PartitionSpec as P

ITERS = 2


def local(
    tiles,
    tile_rows,
    tile_cols,
    tile_count,
    rhs,
    base_cost,
    upper,
    primal,
    dual,
    price_levels,
    scenario_ids,
):
    hp = lax.Precision.HIGHEST
    ntiles = tiles.shape[0]
    row_blocks = rhs.shape[0]
    own_blocks = base_cost.shape[0]
    scenarios = primal.shape[1]
    lanes = primal.shape[2]
    region_blocks = own_blocks * lax.axis_size("col")
    devices = lax.axis_size(("region", "col"))
    live = (jnp.arange(ntiles, dtype=jnp.int32) < tile_count[0]).astype(jnp.float32)
    row_select = (tile_rows[:, None] == jnp.arange(row_blocks, dtype=jnp.int32)[None, :]).astype(
        jnp.float32
    )
    row_live = row_select * live[:, None]
    col_select = (tile_cols[:, None] == jnp.arange(region_blocks, dtype=jnp.int32)[None, :]).astype(
        jnp.float32
    )
    col_live = col_select * live[:, None]
    choose = (
        scenario_ids[:, None] == jnp.arange(price_levels.shape[0], dtype=jnp.int32)[None, :]
    ).astype(jnp.float32)
    factor = jnp.dot(choose, price_levels, precision=hp)
    cost = base_cost[:, None, :] * factor[None, :, :]
    local_a = jnp.sum(jnp.sum(tiles * tiles, axis=(1, 2)) * live)
    local_c = jnp.sum(cost * cost, axis=(0, 2))
    local_b = jnp.sum(rhs * rhs)
    sq_a, sq_c, sq_b = lax.psum((local_a, local_c, local_b), ("region", "col"))
    eta = 0.5 / jnp.sqrt(sq_a / (lanes * row_blocks * devices))
    weight = jnp.sqrt(sq_c) / jnp.sqrt(sq_b)
    width = scenarios * lanes
    for step in range(ITERS):
        tau = (eta / weight)[None, :, None]
        sigma = (eta * weight)[None, :, None]
        dual_rows = jnp.dot(row_select, dual.reshape(row_blocks, width), precision=hp).reshape(
            ntiles, scenarios, lanes
        )
        contrib = jnp.einsum("tij,tsi->tsj", tiles, dual_rows, precision=hp)
        flat_terms = contrib.reshape(ntiles, width)
        partial_value = jnp.dot(col_live.T, flat_terms, precision=hp).reshape(
            region_blocks, scenarios, lanes
        )
        grad = lax.psum_scatter(partial_value, "col", scatter_dimension=0, tiled=True)
        new_primal = jnp.clip(primal - tau * (cost - grad), 0.0, upper[:, None, :])
        point = 2.0 * new_primal - primal
        region_point = lax.all_gather(point, "col", axis=0, tiled=True)
        selected = jnp.dot(
            col_select, region_point.reshape(region_blocks, width), precision=hp
        ).reshape(ntiles, scenarios, lanes)
        image = jnp.einsum("tij,tsj->tsi", tiles, selected, precision=hp)
        product = jnp.dot(row_live.T, image.reshape(ntiles, width), precision=hp).reshape(
            row_blocks, scenarios, lanes
        )
        new_dual = jnp.maximum(dual + sigma * (rhs[:, None, :] - product), 0.0)
        local_x = jnp.sum((new_primal - primal) ** 2, axis=(0, 2))
        local_y = jnp.sum((new_dual - dual) ** 2, axis=(0, 2))
        step_x = lax.psum(local_x, ("region", "col"))
        step_y = lax.psum(local_y, ("region", "col"))
        weight = jnp.sqrt(weight * jnp.sqrt((step_x + 1e-06) / (step_y + 1e-06)))
        primal, dual = (new_primal, new_dual)
    return (primal, dual, weight)


def solution(mesh):
    placed = (
        P(("region", "col"), None, None),
        P(("region", "col")),
        P(("region", "col")),
        P(("region", "col")),
        P(("region", "col"), None),
        P(("region", "col"), None),
        P(("region", "col"), None),
        P(("region", "col"), None, None),
        P(("region", "col"), None, None),
        P(),
        P(),
    )
    return jax.shard_map(
        local,
        mesh=mesh,
        in_specs=placed,
        out_specs=(P(("region", "col"), None, None), P(("region", "col"), None, None), P()),
        check_vma=False,
    )
```

profile of v0, /device:TPU:10, one launch (start us, length us, event | category | flops | bytes accessed | tf_op | source)
XLA Modules:
  0.0 194.1 jit_solution(15329960555821616585)
XLA Ops:
  7.2 0.0 copy-start
  7.2 0.0 copy-start.1
  7.2 0.0 copy-start.7
  7.2 0.0 reduce-scatter.3.cloned.1.call-start
  8.1 1.2 fusion.37
  9.3 0.0 copy-start.10
  9.3 0.0 copy-start.5
  9.3 0.0 copy-start.9
  9.3 0.0 copy-start.3
  9.3 0.0 copy-start.8
  9.3 4.7 %fusion.18 = f32[48,16,128]{2,1,0:T(8,128)S(1)} fusion(f32[48,128,128]{2,1,0:T(8,128)} %param.11, f32[48,16,128]{2,0,1:T(8,128)S(1)} %fusion.37), kind=kOutput, calls=%fused_computation.23 | convolution fusion | flops 150994944 | bytes 3932160 | tf_op jit(solution)/shard_map/tij,tsi->tsj/dot_general | solution.py:57
  14.1 0.0 copy-done.7
  14.1 0.4 fusion.9
  14.5 0.7 copy.80
  15.2 0.0 reduce-scatter.3.cloned.1.call-update
  15.2 0.0 reduce-scatter.5.cloned.1.call-start
  15.2 0.0 copy-done.1
  15.3 0.5 multiply_reduce_fusion
  15.7 0.0 copy-start.6
  15.7 0.0 copy-start.2
  15.7 0.6 fusion.68
  16.3 0.0 copy-done
  16.3 0.0 copy-done.10
  16.3 0.2 fusion.52
  16.5 0.0 copy-done.5
  16.5 0.1 fusion.26
  16.6 0.0 copy-done.9
  16.6 0.6 multiply_reduce_fusion.5
  17.2 41.5 %all-reduce.2 = (f32[16]{0:T(128)S(1)}, f32[]{:T(128)}, f32[]{:T(128)}) all-reduce(f32[16]{0:T(128)S(1)} %fusion.26, f32[]{:T(128)} %fusion.68, f32[]{:T(128)} %multiply_reduce_fusion.5), channel_id=1, replica_groups=mesh['region'=4,'col'=8] {'region','col'}, use_global_device_ids=true, to_apply=%region_6.0 | all-reduce | flops 18 | bytes 144 | tf_op jit(solution)/shard_map/psum | solution.py:47
  60.2 0.0 reduce-scatter.3.cloned.1.call-done
  60.2 0.0 copy-done.3
  60.2 0.0 copy-done.8
  60.2 0.9 multiply_reduce_fusion.4
  61.1 13.1 %all_gather.6 = f32[16,16,128]{2,1,0:T(8,128)S(1)} all-gather(f32[2,16,128]{2,1,0:T(8,128)S(1)} %multiply_subtract_fusion.3), channel_id=1, replica_groups=mesh['region'=4,'col'=8] {'col'}, dimensions={0}, use_global_device_ids=true | all-gather | bytes 147456 | tf_op jit(solution)/shard_map/all_gather | solution.py:65
  74.2 0.4 fusion.23
  74.6 5.0 %fusion.16 = f32[48,16,128]{2,1,0:T(8,128)S(1)} fusion(f32[48,128,128]{2,1,0:T(8,128)S(1)} %copy-done.1, f32[48,16,128]{2,0,1:T(8,128)S(1)} %fusion.23), kind=kOutput, calls=%fused_computation.21 | convolution fusion | flops 150994944 | bytes 3932160 | tf_op jit(solution)/shard_map/tij,tsj->tsi/dot_general | solution.py:69
  79.5 0.0 copy-done.6
  79.5 0.4 fusion.6
  80.0 0.0 copy-done.2
  80.0 0.2 multiply_reduce_fusion.3
  80.2 0.4 fusion.35
  80.6 2.9 %fusion.14 = f32[48,16,128]{2,1,0:T(8,128)S(1)} fusion(f32[48,128,128]{2,1,0:T(8,128)S(1)} %copy-done.1, f32[48,16,128]{2,0,1:T(8,128)S(1)} %fusion.35), kind=kOutput, calls=%fused_computation.19 | convolution fusion | flops 150994944 | bytes 3932160 | tf_op jit(solution)/shard_map/tij,tsi->tsj/dot_general | solution.py:57
  83.4 0.4 fusion.3
  83.9 0.7 copy.87
  84.5 0.0 reduce-scatter.5.cloned.1.call-update
  84.6 40.5 %all-reduce.1 = (f32[16]{0:T(128)S(1)}, f32[16]{0:T(128)S(1)}) all-reduce(f32[16]{0:T(128)S(1)} %get-tuple-element.30, f32[16]{0:T(128)S(1)} %get-tuple-element.28), channel_id=1, replica_groups=mesh['region'=4,'col'=8] {'region','col'}, use_global_device_ids=true, to_apply=%region_11.12 | all-reduce | flops 32 | bytes 256 | tf_op jit(solution)/shard_map/psum | solution.py:77
  125.1 0.0 reduce-scatter.5.cloned.1.call-done
  125.1 0.9 multiply_reduce_fusion.2
  126.0 0.0 copy-start.4
  126.0 12.4 %all_gather.7 = f32[16,16,128]{2,1,0:T(8,128)S(1)} all-gather(f32[2,16,128]{2,1,0:T(8,128)S(1)} %multiply_subtract_fusion.2), channel_id=1, replica_groups=mesh['region'=4,'col'=8] {'col'}, dimensions={0}, use_global_device_ids=true | all-gather | bytes 147456 | tf_op jit(solution)/shard_map/all_gather | solution.py:65
  138.4 0.4 fusion.20
  138.8 5.0 %fusion.12 = f32[48,16,128]{2,1,0:T(8,128)S(1)} fusion(f32[48,128,128]{2,1,0:T(8,128)S(1)} %copy-done.1, f32[48,16,128]{2,0,1:T(8,128)S(1)} %fusion.20), kind=kOutput, calls=%fused_computation.17 | convolution fusion | flops 150994944 | bytes 3932160 | tf_op jit(solution)/shard_map/tij,tsj->tsi/dot_general | solution.py:69
  143.8 0.4 fusion
  144.2 0.8 multiply_reduce_fusion.1
  145.0 41.7 %all-reduce = (f32[16]{0:T(128)S(1)}, f32[16]{0:T(128)S(1)}) all-reduce(f32[16]{0:T(128)S(1)} %get-tuple-element.24, f32[16]{0:T(128)S(1)} %get-tuple-element.22), channel_id=1, replica_groups=mesh['region'=4,'col'=8] {'region','col'}, use_global_device_ids=true, to_apply=%region_16.17 | all-reduce | flops 32 | bytes 256 | tf_op jit(solution)/shard_map/psum | solution.py:77
  186.7 0.5 multiply_sqrt_fusion
  187.2 0.0 copy-done.4
  (6 shorter events, 0.0 us)
Async XLA Ops:
  7.2 9.2 %copy-start = (f32[32,128]{1,0:T(8,128)S(1)}, f32[32,128]{1,0:T(8,128)}, u32[]{:S(2)}) copy-start(f32[32,128]{1,0:T(8,128)} %param.20) | copy-start | bytes 49156
  7.2 8.1 %copy-start.1 = (f32[48,128,128]{2,1,0:T(8,128)S(1)}, f32[48,128,128]{2,1,0:T(8,128)}, u32[]{:S(2)}) copy-start(f32[48,128,128]{2,1,0:T(8,128)} %param.11) | copy-start | bytes 9437188
  7.2 6.9 %copy-start.7 = (s32[48]{0:T(128)S(1)}, s32[48]{0:T(128)}, u32[]{:S(2)}) copy-start(s32[48]{0:T(128)} %param.13) | copy-start | bytes 580
  7.2 53.0 %reduce-scatter.3.cloned.1.call-start = ((), (), s32[]{:S(2)}) async-start(), calls=%async_computation.2 | async-start | bytes 147456 | tf_op jit(solution)/shard_map/reduce_scatter | solution.py:62
  9.3 7.0 %copy-start.10 = (s32[16]{0:T(128)S(1)}, s32[16]{0:T(128)}, u32[]{:S(2)}) copy-start(s32[16]{0:T(128)} %param.21) | copy-start | bytes 196
  9.3 7.2 %copy-start.5 = (f32[2,128]{1,0:T(2,128)S(1)}, f32[2,128]{1,0:T(2,128)}, u32[]{:S(2)}) copy-start(f32[2,128]{1,0:T(2,128)} %param.16) | copy-start | bytes 3076
  9.3 7.3 %copy-start.9 = (f32[2,128]{1,0:T(2,128)S(1)}, f32[2,128]{1,0:T(2,128)}, u32[]{:S(2)}) copy-start(f32[2,128]{1,0:T(2,128)} %param.15) | copy-start | bytes 3076
  9.3 50.9 %copy-start.3 = (f32[2,16,128]{2,1,0:T(8,128)S(1)}, f32[2,16,128]{2,1,0:T(8,128)}, u32[]{:S(2)}) copy-start(f32[2,16,128]{2,1,0:T(8,128)} %param.18) | copy-start | bytes 49156
  9.3 50.9 %copy-start.8 = (f32[2,128]{1,0:T(2,128)S(1)}, f32[2,128]{1,0:T(2,128)}, u32[]{:S(2)}) copy-start(f32[2,128]{1,0:T(2,128)} %param.17) | copy-start | bytes 3076
  15.2 109.9 %reduce-scatter.5.cloned.1.call-start = ((), (), s32[]{:S(2)}) async-start(), calls=%async_computation.3 | async-start | bytes 147456 | tf_op jit(solution)/shard_map/reduce_scatter | solution.py:62
  15.7 63.8 %copy-start.6 = (s32[48]{0:T(128)S(1)}, s32[48]{0:T(128)}, u32[]{:S(2)}) copy-start(s32[48]{0:T(128)} %param.12) | copy-start | bytes 580
  15.7 64.3 %copy-start.2 = (f32[2,16,128]{2,1,0:T(8,128)S(1)}, f32[2,16,128]{2,1,0:T(8,128)}, u32[]{:S(2)}) copy-start(f32[2,16,128]{2,1,0:T(8,128)} %param.19) | copy-start | bytes 49156
  126.0 61.2 %copy-start.4 = (f32[2,16,128]{2,1,0:T(8,128)}, f32[2,16,128]{2,1,0:T(8,128)S(1)}, u32[]{:S(2)}) copy-start(f32[2,16,128]{2,1,0:T(8,128)S(1)} %get-tuple-element.23) | copy-start | bytes 49156
Sparse Core Ops, SparseCore 0:
  15.3 27.7 reduce-scatter.2
  84.7 26.8 reduce-scatter.4
where the time goes:
time: 195 us; the launch traced here: 194 us
  blocking collectives  149 us (76%)
  matrix products  21.7 us (11%)
  between operations  16.4 us (8%)
  other arithmetic  5.15 us (3%)
    psum x2, blocking collectives, local(): step_y = lax.psum(local_y, ('region', 'col'))  82.2 us
    psum x1, blocking collectives, local(): sq_a, sq_c, sq_b = lax.psum((local_a, local_c, local_b), ('region', 'col'))  41.5 us
    all_gather x2, blocking collectives, local(): region_point = lax.all_gather(point, 'col', axis=0, tiled=True)  25.5 us
    dot_general x2, matrix products, local(): image = jnp.einsum('tij,tsj->tsi', tiles, selected, precision=hp)  9.98 us
    dot_general x2, matrix products, local(): contrib = jnp.einsum('tij,tsi->tsj', tiles, dual_rows, precision=hp)  7.59 us
  transfers between devices with their start and end apart: 2, of which 0 were waited for; matrix products, arithmetic and copies ran while one was open for 1% of the time, Pallas kernels for 0%

commit v1 on v0

--- a/solution.py
+++ b/solution.py
@@ -62,7 +62,24 @@
         grad = lax.psum_scatter(partial_value, "col", scatter_dimension=0, tiled=True)
         new_primal = jnp.clip(primal - tau * (cost - grad), 0.0, upper[:, None, :])
         point = 2.0 * new_primal - primal
-        region_point = lax.all_gather(point, "col", axis=0, tiled=True)
+        count, position, span = (lax.axis_size("col"), lax.axis_index("col"), point.shape[0])
+        ahead = [(i, (i + 1) % count) for i in range(count)]
+        behind = [(i, (i - 1) % count) for i in range(count)]
+        out = jnp.zeros((*point.shape[:0], count * span, *point.shape[0 + 1 :]), point.dtype)
+        out = lax.dynamic_update_slice_in_dim(out, point, position * span, axis=0)
+        from_left = from_right = point
+        middle = count // 2
+        for step_2 in range(1, middle + 1):
+            from_left = lax.ppermute(from_left, "col", ahead)
+            out = lax.dynamic_update_slice_in_dim(
+                out, from_left, (position - step_2) % count * span, axis=0
+            )
+            if step_2 < count - middle:
+                from_right = lax.ppermute(from_right, "col", behind)
+                out = lax.dynamic_update_slice_in_dim(
+                    out, from_right, (position + step_2) % count * span, axis=0
+                )
+        region_point = out
         selected = jnp.dot(
             col_select, region_point.reshape(region_blocks, width), precision=hp
         ).reshape(ntiles, scenarios, lanes)

time: 195 us -> 205 us (1.051)
  blocking collectives: 149 us -> 134 us
  waiting for transfers between devices: 0.07 us -> 14.5 us
  starting transfers between devices: 0.08 us -> 11.2 us
    all_gather x2 -> x0, blocking collectives: 25.5 us -> none  [local(): region_point = lax.all_gather(point, 'col', axis=0, tiled=True)]
    ppermute x0 -> x14, waiting for transfers between devices: none -> 14.5 us  [the longest x8 13.6 us: local(): from_left = lax.ppermute(from_left, 'col', ahead)]
    ppermute x0 -> x14, starting transfers between devices: none -> 11.1 us  [the longest x6 10.9 us: local(): from_right = lax.ppermute(from_right, 'col', behind)]
    psum x2, blocking collectives: 82.2 us -> 92.1 us  [local(): step_y = lax.psum(local_y, ('region', 'col'))]
  transfers between devices with their start and end apart: 2 -> 16, of which waited for: 0 -> 11; matrix products, arithmetic and copies ran while one was open for 1% -> 1% of each run, Pallas kernels for 0% -> 0%
where the time goes in v1:
time: 205 us; the launch traced here: 204 us
  blocking collectives  134 us (65%)
  matrix products  21.7 us (11%)
  between operations  16.5 us (8%)
  waiting for transfers between devices  14.5 us (7%)
  starting transfers between devices  11.2 us (5%)
  other arithmetic  5.17 us (3%)
    psum x2, blocking collectives, local(): step_y = lax.psum(local_y, ('region', 'col'))  92.1 us
    psum x1, blocking collectives, local(): sq_a, sq_c, sq_b = lax.psum((local_a, local_c, local_b), ('region', 'col'))  41.5 us
    ppermute x8, waiting for transfers between devices, local(): from_left = lax.ppermute(from_left, 'col', ahead)  13.6 us
    ppermute x6, starting transfers between devices, local(): from_right = lax.ppermute(from_right, 'col', behind)  10.9 us
    dot_general x2, matrix products, local(): image = jnp.einsum('tij,tsj->tsi', tiles, selected, precision=hp)  9.98 us
    dot_general x2, matrix products, local(): contrib = jnp.einsum('tij,tsi->tsj', tiles, dual_rows, precision=hp)  7.59 us
  transfers between devices with their start and end apart: 16, of which 11 were waited for; matrix products, arithmetic and copies ran while one was open for 1% of the time, Pallas kernels for 0%

profile of v1, /device:TPU:10, one launch (start us, length us, event | category | flops | bytes accessed | tf_op | source)
XLA Modules:
  0.0 204.2 jit_solution(16433073791537123829)
XLA Ops:
  7.2 0.0 copy-start
  7.2 0.0 copy-start.1
  7.2 0.0 reduce-scatter.3.cloned.1.call-start
  8.1 1.2 fusion.37
  9.3 0.0 copy-start.10
  9.3 0.0 copy-start.5
  9.3 0.0 copy-start.9
  9.3 0.0 copy-start.3
  9.3 0.0 copy-start.8
  9.3 4.7 %fusion.18 = f32[48,16,128]{2,1,0:T(8,128)S(1)} fusion(f32[48,128,128]{2,1,0:T(8,128)} %param.11, f32[48,16,128]{2,0,1:T(8,128)S(1)} %fusion.37), kind=kOutput, calls=%fused_computation.23 | convolution fusion | flops 150994944 | bytes 3932160 | tf_op jit(solution)/shard_map/tij,tsi->tsj/dot_general | solution.py:57
  14.1 0.4 fusion.9
  14.5 0.7 copy.87
  15.2 0.0 reduce-scatter.3.cloned.1.call-update
  15.2 0.0 reduce-scatter.5.cloned.1.call-start
  15.3 0.5 multiply_reduce_fusion
  15.7 0.0 copy-start.2
  15.7 0.2 fusion.52
  15.9 0.1 fusion.26
  16.1 0.6 fusion.68
  16.7 0.6 multiply_reduce_fusion.5
  17.3 41.5 %all-reduce.2 = (f32[16]{0:T(128)S(1)}, f32[]{:T(128)}, f32[]{:T(128)}) all-reduce(f32[16]{0:T(128)S(1)} %fusion.26, f32[]{:T(128)} %fusion.68, f32[]{:T(128)} %multiply_reduce_fusion.5), channel_id=1, replica_groups=mesh['region'=4,'col'=8] {'region','col'}, use_global_device_ids=true, to_apply=%region_6.0 | all-reduce | flops 18 | bytes 144 | tf_op jit(solution)/shard_map/psum | solution.py:47
  60.2 0.0 reduce-scatter.3.cloned.1.call-done
  60.2 0.9 multiply_reduce_fusion.4
  61.2 0.1 collective-permute-start
  61.2 1.7 collective-permute-start.1
  63.0 1.4 collective-permute-done
  64.4 0.0 collective-permute-done.1
  64.4 2.0 collective-permute-start.3
  66.4 1.1 collective-permute-done.2
  67.6 0.3 collective-permute-done.3
  67.9 1.7 collective-permute-start.5
  69.6 1.1 collective-permute-done.4
  70.7 0.0 collective-permute-start.6
  70.7 0.3 collective-permute-done.5
  71.0 2.9 %collective-permute-done.6 = f32[2,16,128]{2,1,0:T(8,128)S(1)} collective-permute-done((f32[2,16,128]{2,1,0:T(8,128)S(1)}, f32[2,16,128]{2,1,0:T(8,128)S(1)}, u32[]{:S(2)}, u32[]{:S(2)}) %collective-permute-start.6) | collective-permute-done | bytes 16416 | tf_op jit(solution)/shard_map/ppermute | solution.py:73
  73.9 0.4 fusion.23
  74.3 5.0 %fusion.16 = f32[48,16,128]{2,1,0:T(8,128)S(1)} fusion(f32[48,128,128]{2,1,0:T(8,128)S(1)} %copy-done.1, f32[48,16,128]{2,0,1:T(8,128)S(1)} %fusion.23), kind=kOutput, calls=%fused_computation.21 | convolution fusion | flops 150994944 | bytes 3932160 | tf_op jit(solution)/shard_map/tij,tsj->tsi/dot_general | solution.py:86
  79.3 0.4 fusion.6
  79.7 0.2 multiply_reduce_fusion.3
  79.9 0.4 fusion.35
  80.3 2.9 %fusion.14 = f32[48,16,128]{2,1,0:T(8,128)S(1)} fusion(f32[48,128,128]{2,1,0:T(8,128)S(1)} %copy-done.1, f32[48,16,128]{2,0,1:T(8,128)S(1)} %fusion.35), kind=kOutput, calls=%fused_computation.19 | convolution fusion | flops 150994944 | bytes 3932160 | tf_op jit(solution)/shard_map/tij,tsi->tsj/dot_general | solution.py:57
  83.1 0.4 fusion.3
  83.6 0.7 copy.94
  84.3 0.0 reduce-scatter.5.cloned.1.call-update
  84.3 46.6 %all-reduce.1 = (f32[16]{0:T(128)S(1)}, f32[16]{0:T(128)S(1)}) all-reduce(f32[16]{0:T(128)S(1)} %get-tuple-element.29, f32[16]{0:T(128)S(1)} %get-tuple-element.27), channel_id=1, replica_groups=mesh['region'=4,'col'=8] {'region','col'}, use_global_device_ids=true, to_apply=%region_11.12 | all-reduce | flops 32 | bytes 256 | tf_op jit(solution)/shard_map/psum | solution.py:94
  130.9 0.0 reduce-scatter.5.cloned.1.call-done
  131.0 0.9 multiply_reduce_fusion.2
  131.9 0.1 collective-permute-start.7
  132.0 1.7 collective-permute-start.8
  133.7 1.4 collective-permute-done.7
  135.1 0.0 collective-permute-done.8
  135.2 1.7 collective-permute-start.10
  136.9 1.4 collective-permute-done.9
  138.3 0.0 collective-permute-done.10
  138.3 2.0 collective-permute-start.12
  140.3 1.3 collective-permute-done.11
  141.6 0.2 collective-permute-done.12
  141.8 3.0 %collective-permute-done.13 = f32[2,16,128]{2,1,0:T(8,128)S(1)} collective-permute-done((f32[2,16,128]{2,1,0:T(8,128)S(1)}, f32[2,16,128]{2,1,0:T(8,128)S(1)}, u32[]{:S(2)}, u32[]{:S(2)}) %collective-permute-start.13) | collective-permute-done | bytes 16416 | tf_op jit(solution)/shard_map/ppermute | solution.py:73
  144.8 0.4 fusion.20
  145.1 5.0 %fusion.12 = f32[48,16,128]{2,1,0:T(8,128)S(1)} fusion(f32[48,128,128]{2,1,0:T(8,128)S(1)} %copy-done.1, f32[48,16,128]{2,0,1:T(8,128)S(1)} %fusion.20), kind=kOutput, calls=%fused_computation.17 | convolution fusion | flops 150994944 | bytes 3932160 | tf_op jit(solution)/shard_map/tij,tsj->tsi/dot_general | solution.py:86
  150.1 0.4 fusion
  150.6 0.8 multiply_reduce_fusion.1
  151.3 45.5 %all-reduce = (f32[16]{0:T(128)S(1)}, f32[16]{0:T(128)S(1)}) all-reduce(f32[16]{0:T(128)S(1)} %get-tuple-element.21, f32[16]{0:T(128)S(1)} %get-tuple-element.19), channel_id=1, replica_groups=mesh['region'=4,'col'=8] {'region','col'}, use_global_device_ids=true, to_apply=%region_16.17 | all-reduce | flops 32 | bytes 256 | tf_op jit(solution)/shard_map/psum | solution.py:94
  196.9 0.5 multiply_sqrt_fusion
  (41 shorter events, 0.2 us)
Async XLA Ops:
  7.2 8.6 %copy-start = (f32[32,128]{1,0:T(8,128)S(1)}, f32[32,128]{1,0:T(8,128)}, u32[]{:S(2)}) copy-start(f32[32,128]{1,0:T(8,128)} %param.20) | copy-start | bytes 49156
  7.2 8.1 %copy-start.1 = (f32[48,128,128]{2,1,0:T(8,128)S(1)}, f32[48,128,128]{2,1,0:T(8,128)}, u32[]{:S(2)}) copy-start(f32[48,128,128]{2,1,0:T(8,128)} %param.11) | copy-start | bytes 9437188
  7.2 6.9 %copy-start.7 = (s32[48]{0:T(128)S(1)}, s32[48]{0:T(128)}, u32[]{:S(2)}) copy-start(s32[48]{0:T(128)} %param.13) | copy-start | bytes 580
  7.2 53.0 %reduce-scatter.3.cloned.1.call-start = ((), (), s32[]{:S(2)}) async-start(), calls=%async_computation.2 | async-start | bytes 147456 | tf_op jit(solution)/shard_map/reduce_scatter | solution.py:62
  9.3 6.5 %copy-start.10 = (s32[16]{0:T(128)S(1)}, s32[16]{0:T(128)}, u32[]{:S(2)}) copy-start(s32[16]{0:T(128)} %param.21) | copy-start | bytes 196
  9.3 6.6 %copy-start.5 = (f32[2,128]{1,0:T(2,128)S(1)}, f32[2,128]{1,0:T(2,128)}, u32[]{:S(2)}) copy-start(f32[2,128]{1,0:T(2,128)} %param.16) | copy-start | bytes 3076
  9.3 7.4 %copy-start.9 = (f32[2,128]{1,0:T(2,128)S(1)}, f32[2,128]{1,0:T(2,128)}, u32[]{:S(2)}) copy-start(f32[2,128]{1,0:T(2,128)} %param.15) | copy-start | bytes 3076
  9.3 50.9 %copy-start.3 = (f32[2,16,128]{2,1,0:T(8,128)S(1)}, f32[2,16,128]{2,1,0:T(8,128)}, u32[]{:S(2)}) copy-start(f32[2,16,128]{2,1,0:T(8,128)} %param.18) | copy-start | bytes 49156
  9.3 50.9 %copy-start.8 = (f32[2,128]{1,0:T(2,128)S(1)}, f32[2,128]{1,0:T(2,128)}, u32[]{:S(2)}) copy-start(f32[2,128]{1,0:T(2,128)} %param.17) | copy-start | bytes 3076
  15.2 115.7 %reduce-scatter.5.cloned.1.call-start = ((), (), s32[]{:S(2)}) async-start(), calls=%async_computation.3 | async-start | bytes 147456 | tf_op jit(solution)/shard_map/reduce_scatter | solution.py:62
  15.7 63.5 %copy-start.6 = (s32[48]{0:T(128)S(1)}, s32[48]{0:T(128)}, u32[]{:S(2)}) copy-start(s32[48]{0:T(128)} %param.12) | copy-start | bytes 580
  15.7 64.0 %copy-start.2 = (f32[2,16,128]{2,1,0:T(8,128)S(1)}, f32[2,16,128]{2,1,0:T(8,128)}, u32[]{:S(2)}) copy-start(f32[2,16,128]{2,1,0:T(8,128)} %param.19) | copy-start | bytes 49156
  61.2 3.2 %collective-permute-start = (f32[2,16,128]{2,1,0:T(8,128)S(1)}, f32[2,16,128]{2,1,0:T(8,128)S(1)}, u32[]{:S(2)}, u32[]{:S(2)}) collective-permute-start(f32[2,16,128]{2,1,0:T(8,128)S(1)} %get-tuple-element.34), channel_id=1, source_target_pairs={{0,1},{1,2},{2,3},{3,4},{4,5},{5,6},{6,7},{7,0},{8,9},{9,10},{10,1... | collective-permute-start | bytes 49160 | tf_op jit(solution)/shard_map/ppermute | solution.py:73
  61.2 3.2 %collective-permute-start.1 = (f32[2,16,128]{2,1,0:T(8,128)S(1)}, f32[2,16,128]{2,1,0:T(8,128)S(1)}, u32[]{:S(2)}, u32[]{:S(2)}) collective-permute-start(f32[2,16,128]{2,1,0:T(8,128)S(1)} %get-tuple-element.34), channel_id=1, source_target_pairs={{0,7},{1,0},{2,1},{3,2},{4,3},{5,4},{6,5},{7,6},{8,15},{9,8},{10,9... | collective-permute-start | bytes 49160 | tf_op jit(solution)/shard_map/ppermute | solution.py:78
  64.4 3.2 %collective-permute-start.2 = (f32[2,16,128]{2,1,0:T(8,128)S(1)}, f32[2,16,128]{2,1,0:T(8,128)S(1)}, u32[]{:S(2)}, u32[]{:S(2)}) collective-permute-start(f32[2,16,128]{2,1,0:T(8,128)S(1)} %collective-permute-done), channel_id=1, source_target_pairs={{0,1},{1,2},{2,3},{3,4},{4,5},{5,6},{6,7},{7,0},{8,9},{9,10},{10,1... | collective-permute-start | bytes 49160 | tf_op jit(solution)/shard_map/ppermute | solution.py:73
  64.4 3.5 %collective-permute-start.3 = (f32[2,16,128]{2,1,0:T(8,128)S(1)}, f32[2,16,128]{2,1,0:T(8,128)S(1)}, u32[]{:S(2)}, u32[]{:S(2)}) collective-permute-start(f32[2,16,128]{2,1,0:T(8,128)S(1)} %collective-permute-done.1), channel_id=1, source_target_pairs={{0,7},{1,0},{2,1},{3,2},{4,3},{5,4},{6,5},{7,6},{8,15},{9,8},{10,9... | collective-permute-start | bytes 49160 | tf_op jit(solution)/shard_map/ppermute | solution.py:78
  67.6 3.2 %collective-permute-start.4 = (f32[2,16,128]{2,1,0:T(8,128)S(1)}, f32[2,16,128]{2,1,0:T(8,128)S(1)}, u32[]{:S(2)}, u32[]{:S(2)}) collective-permute-start(f32[2,16,128]{2,1,0:T(8,128)S(1)} %collective-permute-done.2), channel_id=1, source_target_pairs={{0,1},{1,2},{2,3},{3,4},{4,5},{5,6},{6,7},{7,0},{8,9},{9,10},{10,1... | collective-permute-start | bytes 49160 | tf_op jit(solution)/shard_map/ppermute | solution.py:73
  67.9 3.2 %collective-permute-start.5 = (f32[2,16,128]{2,1,0:T(8,128)S(1)}, f32[2,16,128]{2,1,0:T(8,128)S(1)}, u32[]{:S(2)}, u32[]{:S(2)}) collective-permute-start(f32[2,16,128]{2,1,0:T(8,128)S(1)} %collective-permute-done.3), channel_id=1, source_target_pairs={{0,7},{1,0},{2,1},{3,2},{4,3},{5,4},{6,5},{7,6},{8,15},{9,8},{10,9... | collective-permute-start | bytes 49160 | tf_op jit(solution)/shard_map/ppermute | solution.py:78
  70.7 3.2 %collective-permute-start.6 = (f32[2,16,128]{2,1,0:T(8,128)S(1)}, f32[2,16,128]{2,1,0:T(8,128)S(1)}, u32[]{:S(2)}, u32[]{:S(2)}) collective-permute-start(f32[2,16,128]{2,1,0:T(8,128)S(1)} %collective-permute-done.4), channel_id=1, source_target_pairs={{0,1},{1,2},{2,3},{3,4},{4,5},{5,6},{6,7},{7,0},{8,9},{9,10},{10,1... | collective-permute-start | bytes 49160 | tf_op jit(solution)/shard_map/ppermute | solution.py:73
  131.9 65.5 %copy-start.4 = (f32[2,16,128]{2,1,0:T(8,128)}, f32[2,16,128]{2,1,0:T(8,128)S(1)}, u32[]{:S(2)}) copy-start(f32[2,16,128]{2,1,0:T(8,128)S(1)} %get-tuple-element.20) | copy-start | bytes 49156
  131.9 3.2 %collective-permute-start.7 = (f32[2,16,128]{2,1,0:T(8,128)S(1)}, f32[2,16,128]{2,1,0:T(8,128)S(1)}, u32[]{:S(2)}, u32[]{:S(2)}) collective-permute-start(f32[2,16,128]{2,1,0:T(8,128)S(1)} %get-tuple-element.26), channel_id=1, source_target_pairs={{0,1},{1,2},{2,3},{3,4},{4,5},{5,6},{6,7},{7,0},{8,9},{9,10},{10,1... | collective-permute-start | bytes 49160 | tf_op jit(solution)/shard_map/ppermute | solution.py:73
  132.0 3.2 %collective-permute-start.8 = (f32[2,16,128]{2,1,0:T(8,128)S(1)}, f32[2,16,128]{2,1,0:T(8,128)S(1)}, u32[]{:S(2)}, u32[]{:S(2)}) collective-permute-start(f32[2,16,128]{2,1,0:T(8,128)S(1)} %get-tuple-element.26), channel_id=1, source_target_pairs={{0,7},{1,0},{2,1},{3,2},{4,3},{5,4},{6,5},{7,6},{8,15},{9,8},{10,9... | collective-permute-start | bytes 49160 | tf_op jit(solution)/shard_map/ppermute | solution.py:78
  135.1 3.2 %collective-permute-start.9 = (f32[2,16,128]{2,1,0:T(8,128)S(1)}, f32[2,16,128]{2,1,0:T(8,128)S(1)}, u32[]{:S(2)}, u32[]{:S(2)}) collective-permute-start(f32[2,16,128]{2,1,0:T(8,128)S(1)} %collective-permute-done.7), channel_id=1, source_target_pairs={{0,1},{1,2},{2,3},{3,4},{4,5},{5,6},{6,7},{7,0},{8,9},{9,10},{10,1... | collective-permute-start | bytes 49160 | tf_op jit(solution)/shard_map/ppermute | solution.py:73
  135.2 3.2 %collective-permute-start.10 = (f32[2,16,128]{2,1,0:T(8,128)S(1)}, f32[2,16,128]{2,1,0:T(8,128)S(1)}, u32[]{:S(2)}, u32[]{:S(2)}) collective-permute-start(f32[2,16,128]{2,1,0:T(8,128)S(1)} %collective-permute-done.8), channel_id=1, source_target_pairs={{0,7},{1,0},{2,1},{3,2},{4,3},{5,4},{6,5},{7,6},{8,15},{9,8},{10,9... | collective-permute-start | bytes 49160 | tf_op jit(solution)/shard_map/ppermute | solution.py:78
  138.3 3.3 %collective-permute-start.11 = (f32[2,16,128]{2,1,0:T(8,128)S(1)}, f32[2,16,128]{2,1,0:T(8,128)S(1)}, u32[]{:S(2)}, u32[]{:S(2)}) collective-permute-start(f32[2,16,128]{2,1,0:T(8,128)S(1)} %collective-permute-done.9), channel_id=1, source_target_pairs={{0,1},{1,2},{2,3},{3,4},{4,5},{5,6},{6,7},{7,0},{8,9},{9,10},{10,1... | collective-permute-start | bytes 49160 | tf_op jit(solution)/shard_map/ppermute | solution.py:73
  138.3 3.5 %collective-permute-start.12 = (f32[2,16,128]{2,1,0:T(8,128)S(1)}, f32[2,16,128]{2,1,0:T(8,128)S(1)}, u32[]{:S(2)}, u32[]{:S(2)}) collective-permute-start(f32[2,16,128]{2,1,0:T(8,128)S(1)} %collective-permute-done.10), channel_id=1, source_target_pairs={{0,7},{1,0},{2,1},{3,2},{4,3},{5,4},{6,5},{7,6},{8,15},{9,8},{10,9... | collective-permute-start | bytes 49160 | tf_op jit(solution)/shard_map/ppermute | solution.py:78
  141.6 3.2 %collective-permute-start.13 = (f32[2,16,128]{2,1,0:T(8,128)S(1)}, f32[2,16,128]{2,1,0:T(8,128)S(1)}, u32[]{:S(2)}, u32[]{:S(2)}) collective-permute-start(f32[2,16,128]{2,1,0:T(8,128)S(1)} %collective-permute-done.11), channel_id=1, source_target_pairs={{0,1},{1,2},{2,3},{3,4},{4,5},{5,6},{6,7},{7,0},{8,9},{9,10},{10,1... | collective-permute-start | bytes 49160 | tf_op jit(solution)/shard_map/ppermute | solution.py:73
Sparse Core Ops, SparseCore 0:
  15.3 27.7 reduce-scatter.2
  84.4 31.3 reduce-scatter.4
